TPU v7x, 32 devices: a whole 2x2x4 slice. The times are simulated.
32 devices in a mesh: expert: 4 (over z), shard: 8 (over y, x, core).
Axes of the slice: x: 2, y: 2, z: 4, core: 2. Of those that a mesh axis runs over, the one named last changes fastest.
Arguments:
- tokens: bfloat16 [18912, 768], P(('expert', 'shard')), may hold values from -6 to 6
- image_counts: int32 [4, 8], P('expert', 'shard'), may hold values from 1 to 3, as said below
- routes: int32 [18912, 2], P(('expert', 'shard')), may hold values from 0 to 3, all different within a row; in each aligned block of 591 rows (0 to 590, 591 to 1181, ...) at most 376 rows name the same one
- w_qkv: bfloat16 [768, 2304], P('shard'), may hold values from -0.21875 to 0.21875
- w_out: bfloat16 [768, 768], P('shard'), may hold values from -1.5 to 1.5
- w_router: bfloat16 [768, 4], P('shard'), may hold values from -0.15625 to 0.15625
- gain_attn: bfloat16 [768], P('shard'), may hold values from 0.25 to 1.75
- gain_moe: bfloat16 [768], P('shard'), may hold values from 0.25 to 1.75
- w_in: bfloat16 [4, 768, 3072], P('expert', 'shard'), may hold values from -0.21875 to 0.21875
- w_back: bfloat16 [4, 3072, 768], P('expert', 'shard'), may hold values from -0.625 to 0.625
- cotangent: bfloat16 [18912, 768], P(('expert', 'shard')), may hold values from -6 to 6
Outputs:
- output: bfloat16 [18912, 768], P(('expert', 'shard'))
- grad_tokens: bfloat16 [18912, 768], P(('expert', 'shard'))
- grad_w_qkv: float32 [768, 2304], P('shard')
- grad_w_out: float32 [768, 768], P('shard')
- grad_w_router: float32 [768, 4], P('shard')
- grad_gain_attn: float32 [768], P('shard')
- grad_gain_moe: float32 [768], P('shard')
- grad_w_in: float32 [4, 768, 3072], P('expert', 'shard')
- grad_w_back: float32 [4, 3072, 768], P('expert', 'shard')
Inputs may be any that keep to these rules, and one draw needn't show every extreme that they name: `image_counts`: each device holds between 1 and 3 live images; some device holds 3 and some holds 1. `routes`: the two experts of a token differ; among the rows of one device at most 376 name any one expert.
All inputs are finite; a program needn't handle non-finite values.
Results may differ from a plain program's by a relative error of at most 0.024.
Values may be sent and summed in bfloat16 or wider, within the bound.
No kernel may reach another device: no remote copies, remote signals or barrier semaphores. Data moves between devices by JAX's collectives and lax.ppermute only.
A program may use at most 256 MiB of HBM per device.

v0:
```python
import jax
import jax.numpy as jnp
from jax import lax
from jax.sharding import PartitionSpec as P

H = 12
HD = 64
SEQ = 197
EPSILON = 1e-06
ROW_CONTRACT = (((0,), (0,)), ((), ()))
COL_CONTRACT = (((1,), (1,)), ((), ()))


def layer_norm(values, norm_gain):
    row_mean = jnp.mean(values, axis=-1, keepdims=True)
    centered = values - row_mean
    variance = jnp.mean(centered * centered, axis=-1, keepdims=True)
    return centered * lax.rsqrt(variance + EPSILON) * norm_gain


def normalize_rows(scores):
    row_top = jnp.max(scores, axis=-1, keepdims=True)
    exp_scores = jnp.exp(scores - row_top)
    return exp_scores / jnp.sum(exp_scores, axis=-1, keepdims=True)


def gelu_exact(values):
    return jax.nn.gelu(values, approximate=False)


def shards(
    tokens,
    image_counts,
    routes,
    w_qkv,
    w_out,
    w_router,
    gain_attn,
    gain_moe,
    w_in,
    w_back,
    cotangent,
):
    rows, width = tokens.shape
    experts = lax.axis_size("expert")
    capacity = 8 * (5 * rows // (16 * experts)) + 8
    overflow = experts * capacity
    images = rows // SEQ
    qkv_cols = w_qkv.shape[1]
    n_route = w_router.shape[1]
    ff = w_in.shape[2]
    score_scale = HD ** (-0.5)
    row_ids = jnp.arange(rows, dtype=jnp.int32)
    live_int = (row_ids // SEQ < image_counts[0, 0]).astype(jnp.int32)
    live_rows = live_int.astype(jnp.float32)
    dense_local = jnp.concatenate(
        [w_qkv, w_out, w_router, gain_attn[:, None], gain_moe[:, None]], axis=1
    )
    dense_full = lax.all_gather(dense_local, "shard", axis=0, tiled=True)
    full_qkv = dense_full[:, :qkv_cols]
    full_out = dense_full[:, qkv_cols : qkv_cols + width]
    full_router = dense_full[:, qkv_cols + width : qkv_cols + width + n_route]
    gain_one = dense_full[:, -2].astype(jnp.float32)
    gain_two = dense_full[:, -1].astype(jnp.float32)
    back_rows = w_back.shape[1]
    expert_local = jnp.stack([w_in[0], w_back[0].reshape(back_rows * width // ff, ff)], axis=0)
    expert_full = lax.all_gather(expert_local, "shard", axis=1, tiled=True)
    expert_first = expert_full[0]
    expert_second = expert_full[1].reshape(ff, width)
    token_f = tokens.astype(jnp.float32)
    attn_in = layer_norm(token_f, gain_one).astype(jnp.bfloat16)
    projected = jnp.dot(attn_in, full_qkv, preferred_element_type=jnp.float32).astype(jnp.bfloat16)
    split_heads = projected.reshape(images, SEQ, 3, H, HD)
    queries = split_heads[:, :, 0]
    keys_part = split_heads[:, :, 1]
    values_part = split_heads[:, :, 2]
    scores = (
        jnp.einsum("ishd,ithd->ihst", queries, keys_part, preferred_element_type=jnp.float32)
        * score_scale
    )
    row_top = jnp.max(scores, axis=-1, keepdims=True)
    log_total = row_top + jnp.log(jnp.sum(jnp.exp(scores - row_top), axis=-1, keepdims=True))
    attn_probs = jnp.exp(scores - log_total)
    probs_low = attn_probs.astype(jnp.bfloat16)
    mixed_rows = (
        jnp.einsum("ihst,ithd->ishd", probs_low, values_part, preferred_element_type=jnp.float32)
        .reshape(rows, width)
        .astype(jnp.bfloat16)
    )
    hidden_state = token_f + jnp.dot(mixed_rows, full_out, preferred_element_type=jnp.float32)
    moe_in = layer_norm(hidden_state, gain_two).astype(jnp.bfloat16)
    logits = jnp.dot(moe_in, full_router, preferred_element_type=jnp.float32)
    router_probs = normalize_rows(logits)
    expert_ids = jnp.arange(experts, dtype=jnp.int32)
    choose = (routes[:, :, None] == expert_ids).astype(jnp.float32)
    chosen = jnp.sum(choose * router_probs[:, None, :], axis=2)
    pick_table = (routes[:, :, None] == expert_ids).astype(jnp.int32) * live_int[:, None, None]
    flat_picks = pick_table.reshape(rows * 2, experts)
    before = jnp.cumsum(flat_picks, axis=0) - flat_picks
    slot_index = jnp.sum(before * flat_picks, axis=1).reshape(rows, 2)
    position = jnp.where(live_int[:, None] > 0, routes * capacity + slot_index, overflow)
    half_cap = 8 * ((capacity + 15) // 16)
    chunk_sizes = [half_cap, capacity - half_cap] if capacity > half_cap else [capacity]
    chunk_starts = [sum(chunk_sizes[:k]) for k in range(len(chunk_sizes))]
    slot_ids = jnp.concatenate(
        [
            (
                jnp.arange(experts, dtype=jnp.int32)[:, None] * capacity
                + start
                + jnp.arange(size, dtype=jnp.int32)[None, :]
            ).reshape(-1)
            for start, size in zip(chunk_starts, chunk_sizes)
        ]
    )[:, None]
    take_first = (slot_ids == position[None, :, 0]).astype(jnp.bfloat16)
    take_second = (slot_ids == position[None, :, 1]).astype(jnp.bfloat16)
    grad_out = cotangent.astype(jnp.float32) * live_rows[:, None]
    weighted = chosen * live_rows[:, None]
    grad_picked = (weighted[:, :, None] * grad_out[:, None, :]).astype(jnp.bfloat16)
    sent_rows = jnp.dot(
        take_first + take_second, moe_in, preferred_element_type=jnp.float32
    ).astype(jnp.bfloat16)
    sent_grad = (
        jnp.dot(take_first, grad_picked[:, 0], preferred_element_type=jnp.float32)
        + jnp.dot(take_second, grad_picked[:, 1], preferred_element_type=jnp.float32)
    ).astype(jnp.bfloat16)
    outgoing = jnp.concatenate([sent_rows, sent_grad], axis=1)
    grad_first = None
    grad_second = None
    returned_parts = []
    for start, size in zip(chunk_starts, chunk_sizes):
        arrived = lax.all_to_all(
            outgoing[experts * start : experts * (start + size)].reshape(experts, size, 2 * width),
            "expert",
            split_axis=0,
            concat_axis=0,
            tiled=True,
        ).reshape(experts * size, 2 * width)
        flat_arrived = arrived[:, :width]
        flat_grad = arrived[:, width:]
        pre_act = jnp.dot(flat_arrived, expert_first, preferred_element_type=jnp.float32)
        activated, gelu_back = jax.vjp(gelu_exact, pre_act)
        activated = activated.astype(jnp.bfloat16)
        produced = jnp.dot(activated, expert_second, preferred_element_type=jnp.float32).astype(
            jnp.bfloat16
        )
        hidden_grad = lax.dot_general(
            flat_grad, expert_second, COL_CONTRACT, preferred_element_type=jnp.float32
        )
        pre_grad = gelu_back(hidden_grad)[0].astype(jnp.bfloat16)
        row_grad = lax.dot_general(
            pre_grad, expert_first, COL_CONTRACT, preferred_element_type=jnp.float32
        ).astype(jnp.bfloat16)
        part_second = lax.dot_general(
            activated, flat_grad, ROW_CONTRACT, preferred_element_type=jnp.float32
        )
        part_first = lax.dot_general(
            flat_arrived, pre_grad, ROW_CONTRACT, preferred_element_type=jnp.float32
        )
        grad_first = part_first if grad_first is None else grad_first + part_first
        grad_second = part_second if grad_second is None else grad_second + part_second
        returning = jnp.concatenate([produced, row_grad], axis=1).reshape(experts, size, 2 * width)
        returned_parts.append(
            lax.all_to_all(returning, "expert", split_axis=0, concat_axis=0, tiled=True)
        )
    expert_grads = jnp.stack([grad_first, grad_second.reshape(width, ff)], axis=0).astype(
        jnp.bfloat16
    )
    expert_share = lax.psum_scatter(expert_grads, "shard", scatter_dimension=1, tiled=True).astype(
        jnp.float32
    )
    grad_in_share = expert_share[0][None]
    grad_back_share = expert_share[1].reshape(back_rows, width)[None]
    returned = jnp.concatenate([part.reshape(-1, 2 * width) for part in returned_parts], axis=0)
    picked_first = lax.dot_general(
        take_first, returned, ROW_CONTRACT, preferred_element_type=jnp.float32
    )
    picked_second = lax.dot_general(
        take_second, returned, ROW_CONTRACT, preferred_element_type=jnp.float32
    )
    moe_out = (
        weighted[:, 0:1] * picked_first[:, :width] + weighted[:, 1:2] * picked_second[:, :width]
    )
    output = (live_rows[:, None] * (hidden_state + moe_out)).astype(jnp.bfloat16)
    grad_chosen = (
        jnp.stack(
            [
                jnp.sum(grad_out * picked_first[:, :width], axis=1),
                jnp.sum(grad_out * picked_second[:, :width], axis=1),
            ],
            axis=1,
        )
        * live_rows[:, None]
    )
    expert_part = (picked_first[:, width:] + picked_second[:, width:]) * live_rows[:, None]
    prob_sum = jnp.sum(choose * grad_chosen[:, :, None], axis=1)
    logit_grad = (
        router_probs * (prob_sum - jnp.sum(router_probs * prob_sum, axis=-1, keepdims=True))
    ).astype(jnp.bfloat16)
    grad_router = lax.dot_general(
        moe_in, logit_grad, ROW_CONTRACT, preferred_element_type=jnp.float32
    )
    moe_in_grad = expert_part + lax.dot_general(
        logit_grad, full_router, COL_CONTRACT, preferred_element_type=jnp.float32
    )
    norm_value, norm_back = jax.vjp(layer_norm, hidden_state, gain_two)
    state_part, grad_gain_two = norm_back(moe_in_grad)
    state_grad = grad_out + state_part
    branch_grad = state_grad.astype(jnp.bfloat16)
    grad_wout = lax.dot_general(
        mixed_rows, branch_grad, ROW_CONTRACT, preferred_element_type=jnp.float32
    )
    mixed_grad = lax.dot_general(
        branch_grad, full_out, COL_CONTRACT, preferred_element_type=jnp.float32
    )
    mixed_grad = mixed_grad.astype(jnp.bfloat16).reshape(images, SEQ, H, HD)
    grad_values = jnp.einsum(
        "ihst,ishd->ithd", probs_low, mixed_grad, preferred_element_type=jnp.float32
    )
    prob_grad = jnp.einsum(
        "ishd,ithd->ihst", mixed_grad, values_part, preferred_element_type=jnp.float32
    )
    score_grad = (
        attn_probs * (prob_grad - jnp.sum(attn_probs * prob_grad, axis=-1, keepdims=True))
    ).astype(jnp.bfloat16)
    grad_queries = (
        jnp.einsum("ihst,ithd->ishd", score_grad, keys_part, preferred_element_type=jnp.float32)
        * score_scale
    )
    grad_keys = (
        jnp.einsum("ihst,ishd->ithd", score_grad, queries, preferred_element_type=jnp.float32)
        * score_scale
    )
    projected_grad = (
        jnp.stack([grad_queries, grad_keys, grad_values], axis=2)
        .reshape(rows, 3 * width)
        .astype(jnp.bfloat16)
    )
    grad_qkv = lax.dot_general(
        attn_in, projected_grad, ROW_CONTRACT, preferred_element_type=jnp.float32
    )
    attn_in_grad = lax.dot_general(
        projected_grad, full_qkv, COL_CONTRACT, preferred_element_type=jnp.float32
    )
    first_value, first_back = jax.vjp(layer_norm, token_f, gain_one)
    token_part, grad_gain_one = first_back(attn_in_grad)
    grad_tokens = (state_grad + token_part).astype(jnp.bfloat16)
    dense_grads = jnp.concatenate(
        [grad_qkv, grad_wout, grad_router, grad_gain_one[:, None], grad_gain_two[:, None]], axis=1
    ).astype(jnp.bfloat16)
    dense_share = lax.psum_scatter(dense_grads, "shard", scatter_dimension=0, tiled=True)
    dense_total = lax.psum(dense_share, "expert").astype(jnp.float32)
    return (
        output,
        grad_tokens,
        dense_total[:, :qkv_cols],
        dense_total[:, qkv_cols : qkv_cols + width],
        dense_total[:, qkv_cols + width : qkv_cols + width + n_route],
        dense_total[:, -2],
        dense_total[:, -1],
        grad_in_share,
        grad_back_share,
    )


def solution(mesh):
    return jax.shard_map(
        shards,
        mesh=mesh,
        in_specs=(
            P(("expert", "shard"), None),
            P("expert", "shard"),
            P(("expert", "shard"), None),
            P("shard", None),
            P("shard", None),
            P("shard", None),
            P("shard"),
            P("shard"),
            P("expert", "shard", None),
            P("expert", "shard", None),
            P(("expert", "shard"), None),
        ),
        out_specs=(
            P(("expert", "shard"), None),
            P(("expert", "shard"), None),
            P("shard", None),
            P("shard", None),
            P("shard", None),
            P("shard"),
            P("shard"),
            P("expert", "shard", None),
            P("expert", "shard", None),
        ),
        check_vma=False,
    )
```

profile of v0, /device:TPU:0, one launch (start us, length us, event | category | flops | bytes accessed | tf_op | source)
XLA Modules:
  0.0 615.3 jit_solution(7871678161351734495)
XLA Ops:
  21.7 32.4 %all-gather.3.cloned.1.call-done = bf16[768,3078]{1,0:T(8,128)(2,1)} async-done(((bf16[96,3078]{1,0:T(8,128)(2,1)}), bf16[768,3078]{1,0:T(8,128)(2,1)}) %all-gather.3.cloned.1.call-update) | async-done | bytes 4727824 | tf_op jit(solution)/shard_map/all_gather | solution.py:59
  61.5 9.3 %reshape.271 = bf16[3,197,3,12,64]{4,3,2,1,0:T(8,128)(2,1)} reshape(bf16[591,2304]{1,0:T(8,128)(2,1)} %convolution_convert_fusion.1) | data formatting | bytes 5446656 | tf_op jit(solution)/shard_map/reshape | solution.py:73
  70.9 6.6 %fusion.117 = (bf16[3,197,1,12,64]{4,3,2,1,0:T(8,128)(2,1)}, bf16[3,197,1,12,64]{4,3,2,1,0:T(8,128)(2,1)}, bf16[3,197,1,12,64]{4,3,2,1,0:T(8,128)(2,1)}) fusion(bf16[3,197,3,12,64]{4,3,2,1,0:T(8,128)(2,1)} %reshape.271), kind=kLoop, calls=%fused_computation.219 | loop fusion | bytes 5446656 | tf_op jit(solution)/shard_map/slice | solution.py:74
  128.1 8.5 %reshape_squeeze.3 = bf16[3072,768]{1,0:T(8,128)(2,1)} reshape(bf16[1,768,3072]{2,1,0:T(8,128)(2,1)} %slice.165) | data formatting | bytes 9437184 | tf_op jit(solution)/shard_map/reshape;squeeze | solution.py:69
  136.6 36.2 %all-to-all-done.2 = bf16[4,184,1536]{2,1,0:T(8,128)(2,1)} async-done(((bf16[4,184,1536]{2,1,0:T(8,128)(2,1)}), bf16[4,184,1536]{2,1,0:T(8,128)(2,1)}, u32[]{:S(2)}, u32[]{:S(2)}) %all-to-all-start.2) | async-done | bytes 2261024 | tf_op jit(solution)/shard_map/all_to_all | solution.py:132
  176.9 25.8 %multiply_convert_fusion.1 = (bf16[736,3072]{1,0:T(8,128)(2,1)S(1)}, f32[736,3072]{1,0:T(8,128)}, f32[736,3072]{1,0:T(8,128)}) fusion(bf16[2,768,3072]{2,1,0:T(8,128)(2,1)} %all-gather.5.cloned.1.call-done, bf16[736,1536]{1,0:T(8,128)(2,1)} %bitcast.16), kind=kOutput, calls=%fused_computation.23 | convolution fusion | flops 3619848192 | bytes 28459008 | tf_op jit(solution)/shard_map/dot_general | solution.py:141
  206.4 11.8 %add_convert_fusion.3 = bf16[736,3072]{1,0:T(8,128)(2,1)} fusion(f32[736,3072]{1,0:T(8,128)} %get-tuple-element.73, f32[736,3072]{1,0:T(8,128)} %get-tuple-element.86, bf16[3072,768]{1,0:T(8,128)(2,1)S(1)} %copy-done.22, bf16[736,1536]{1,0:T(8,128)(2,1)} %bitcast.16), kind=kOutput, calls=%fused_computation.22 | convolution fusion | flops 3504537600 | bytes 28459008 | tf_op jit(solution)/shard_map/dot_general | solution.py:147
  218.2 6.1 fusion.58
  235.0 26.3 %multiply_convert_fusion = (bf16[768,3072]{1,0:T(8,128)(2,1)S(1)}, f32[768,3072]{1,0:T(8,128)}, f32[768,3072]{1,0:T(8,128)}) fusion(bf16[2,768,3072]{2,1,0:T(8,128)(2,1)} %all-gather.5.cloned.1.call-done, bf16[768,1536]{1,0:T(8,128)(2,1)S(1)} %bitcast.113), kind=kOutput, calls=%fused_computation.7 | convolution fusion | flops 3777232896 | bytes 29491200 | tf_op jit(solution)/shard_map/dot_general | solution.py:141
  261.2 8.1 %convolution_convert_fusion.4 = bf16[768,768]{0,1:T(8,128)(2,1)S(1)} fusion(bf16[768,3072]{1,0:T(8,128)(2,1)S(1)} %get-tuple-element.70, bf16[3072,768]{1,0:T(8,128)(2,1)} %reshape_squeeze.3), kind=kOutput, calls=%fused_computation.119 | convolution fusion | flops 3624468480 | bytes 10616832 | tf_op jit(solution)/shard_map/dot_general | solution.py:144
  269.4 11.0 %add_convert_fusion.2 = bf16[768,3072]{1,0:T(8,128)(2,1)S(1)} fusion(f32[768,3072]{1,0:T(8,128)} %get-tuple-element.71, f32[768,3072]{1,0:T(8,128)} %get-tuple-element.87, bf16[3072,768]{1,0:T(8,128)(2,1)} %reshape_squeeze.3, bf16[768,1536]{1,0:T(8,128)(2,1)S(1)} %bitcast.114), kind=kOutput, calls=%fused_computation.6 | convolution fusion | flops 3656908800 | bytes 29491200 | tf_op jit(solution)/shard_map/dot_general | solution.py:147
  280.4 8.0 %fusion.57 = bf16[768,768]{0,1:T(8,128)(2,1)S(1)} fusion(bf16[768,3072]{1,0:T(8,128)(2,1)S(1)} %add_convert_fusion.2, bf16[2,768,3072]{2,1,0:T(8,128)(2,1)} %all-gather.5.cloned.1.call-done), kind=kOutput, calls=%fused_computation.117 | convolution fusion | flops 3624468480 | bytes 10616832 | tf_op jit(solution)/shard_map/dot_general | solution.py:151
  296.6 52.4 %all-to-all-done.1 = bf16[4,192,1536]{2,1,0:T(8,128)(2,1)S(1)} async-done(((bf16[4,192,1536]{2,1,0:T(8,128)(2,1)}), bf16[4,192,1536]{2,1,0:T(8,128)(2,1)S(1)}, u32[]{:S(2)}, u32[]{:S(2)}) %all-to-all-start.1) | async-done | bytes 2359328 | tf_op jit(solution)/shard_map/all_to_all | solution.py:164
  397.9 9.9 %convert_element_type.172 = bf16[591,2304]{0,1:T(8,128)(2,1)} reshape(bf16[3,197,3,12,64]{1,0,4,3,2:T(4,128)(2,1)} %copy.137) | data formatting | bytes 5446656 | tf_op jit(solution)/shard_map/convert_element_type | solution.py:237
  407.9 7.0 %convolution_convert_fusion = bf16[768,2304]{1,0:T(8,128)(2,1)} fusion(bf16[591,2304]{0,1:T(8,128)(2,1)} %convert_element_type.172, bf16[591,768]{1,0:T(8,128)(2,1)S(1)} %copy-done.9, f32[768]{0:T(1024)S(1)} %copy-done.55, f32[591]{0:T(1024)S(1)} %copy-done.57, f32[591]{0:T(1024)S(1)} %copy-done.47), kind=kOutput, calls=%fused_computation.52 | convolution fusion | flops 2095554816 | bytes 7177848 | tf_op jit(solution)/shard_map/dot_general | solution.py:239
  421.1 8.4 %concatenate.32 = bf16[768,3078]{1,0:T(8,128)(2,1)} concatenate(bf16[768,2304]{1,0:T(8,128)(2,1)} %convolution_convert_fusion, bf16[768,768]{1,0:T(8,128)(2,1)} %convolution_convert_fusion.6, bf16[768,4]{1,0:T(8,128)(2,1)S(1)} %copy.139, bf16[768,1]{1,0:T(8,128)(2,1)S(1)} %broadcast_in_dim.40, bf16[768,1]{1,0:T(8,128)(2,1)S(1)} %broadcast_in_dim.41), dimensions={1} | concatenate | bytes 9455616 | tf_op jit(solution)/shard_map/concatenate | solution.py:248
  437.2 9.2 %fusion.78 = f32[768,3072]{1,0:T(8,128)} fusion(bf16[768,3072]{1,0:T(8,128)(2,1)} %copy-done.23, bf16[768,1536]{1,0:T(8,128)(2,1)S(1)} %bitcast.116), kind=kOutput, calls=%fused_computation.144 | convolution fusion | flops 3623878656 | bytes 15335424 | tf_op jit(solution)/shard_map/dot_general | solution.py:157
  446.4 8.7 %add_convert_fusion = bf16[3072,768]{1,0:T(8,128)(2,1)} fusion(f32[3072,768]{1,0:T(8,128)S(1)} %fusion.72, bf16[736,3072]{1,0:T(8,128)(2,1)} %copy-done.65, bf16[736,1536]{1,0:T(8,128)(2,1)} %bitcast.16), kind=kOutput, calls=%fused_computation.4 | convolution fusion | flops 3477602304 | bytes 19808256 | tf_op jit(solution)/shard_map/dot_general | solution.py:154
  455.0 27.7 %reduce-scatter.3.cloned.1.call-done = bf16[96,3078]{1,0:T(8,128)(2,1)} async-done(((bf16[768,3078]{1,0:T(8,128)(2,1)}), bf16[96,3078]{1,0:T(8,128)(2,1)}) %reduce-scatter.3.cloned.1.call-update) | async-done | bytes 590992 | tf_op jit(solution)/shard_map/reduce_scatter | solution.py:251
  482.8 11.5 %fusion.21 = bf16[1,768,3072]{2,1,0:T(8,128)(2,1)} fusion(f32[768,3072]{1,0:T(8,128)} %fusion.78, bf16[736,3072]{1,0:T(8,128)(2,1)} %add_convert_fusion.3, bf16[736,1536]{1,0:T(8,128)(2,1)} %bitcast.16), kind=kOutput, calls=%fused_computation.60 | convolution fusion | flops 3477602304 | bytes 19808256 | tf_op jit(solution)/shard_map/dot_general | solution.py:157
  494.3 8.7 %stack_reshape.4 = bf16[1,768,3072]{2,1,0:T(8,128)(2,1)} reshape(bf16[3072,768]{1,0:T(8,128)(2,1)} %add_convert_fusion) | data formatting | bytes 9437184 | tf_op jit(solution)/shard_map/stack;reshape | solution.py:166
  503.1 8.3 %pad_maximum_fusion = bf16[2,768,3072]{2,1,0:T(8,128)(2,1)} fusion(bf16[1,768,3072]{2,1,0:T(8,128)(2,1)} %stack_reshape.4, bf16[1,768,3072]{2,1,0:T(8,128)(2,1)} %fusion.21), kind=kLoop, calls=%fused_computation.3 | loop fusion | flops 4718592 | bytes 18874368 | tf_op jit(solution)/shard_map/stack | solution.py:166
  516.2 8.5 %all-reduce.3.cloned.1.call-done = bf16[96,3078]{1,0:T(8,128)(2,1)} async-done(((bf16[96,3078]{1,0:T(8,128)(2,1)}), bf16[96,3078]{1,0:T(8,128)(2,1)}) %all-reduce.3.cloned.1.call-update) | async-done | bytes 590992 | tf_op jit(solution)/shard_map/psum | solution.py:252
  531.6 72.8 %reduce-scatter.5.cloned.1.call-done = bf16[2,96,3072]{2,1,0:T(8,128)(2,1)} async-done(((bf16[2,768,3072]{2,1,0:T(8,128)(2,1)}), bf16[2,96,3072]{2,1,0:T(8,128)(2,1)}) %reduce-scatter.5.cloned.1.call-update) | async-done | bytes 1179664 | tf_op jit(solution)/shard_map/reduce_scatter | solution.py:169
  (274 shorter events, 175.9 us)
Async XLA Ops:
  7.2 46.9 %all-gather.3.cloned.1.call-start = ((), (), s32[]{:S(2)}) async-start(), calls=%async_computation.6 | async-start | bytes 5529600 | tf_op jit(solution)/shard_map/all_gather | solution.py:59
  11.6 111.7 %all-gather.5.cloned.1.call-start = ((), (), s32[]{:S(2)}) async-start(), calls=%async_computation.7 | async-start | bytes 10616832 | tf_op jit(solution)/shard_map/all_gather | solution.py:67
  19.3 85.8 %copy-start.30 = (f32[591]{0:T(1024)}, f32[591]{0:T(1024)S(1)}, u32[]{:S(2)}) copy-start(f32[591]{0:T(1024)S(1)} %fusion.106) | copy-start | bytes 7096
  19.4 90.9 %copy-start.58 = (s32[1504]{0:T(1024)}, s32[1504]{0:T(1024)S(1)}, u32[]{:S(2)}) copy-start(s32[1504]{0:T(1024)S(1)} %pad_add_fusion) | copy-start | bytes 18052
  19.4 88.7 %copy-start.60 = (s32[591]{0:T(1024)}, s32[591]{0:T(1024)S(1)}, u32[]{:S(2)}) copy-start(s32[591]{0:T(1024)S(1)} %get-tuple-element.67) | copy-start | bytes 7096
  19.4 90.9 %copy-start.62 = (s32[591]{0:T(1024)}, s32[591]{0:T(1024)S(1)}, u32[]{:S(2)}) copy-start(s32[591]{0:T(1024)S(1)} %get-tuple-element.66) | copy-start | bytes 7096
  19.7 41.8 %copy-start.46 = (f32[591]{0:T(1024)}, f32[591]{0:T(1024)S(1)}, u32[]{:S(2)}) copy-start(f32[591]{0:T(1024)S(1)} %broadcast_multiply_fusion.2) | copy-start | bytes 7096
  20.1 41.4 %copy-start.50 = (f32[591]{0:T(1024)}, f32[591]{0:T(1024)S(1)}, u32[]{:S(2)}) copy-start(f32[591]{0:T(1024)S(1)} %fusion.53) | copy-start | bytes 7096
  20.1 41.4 %copy-start.56 = (f32[591]{0:T(1024)}, f32[591]{0:T(1024)S(1)}, u32[]{:S(2)}) copy-start(f32[591]{0:T(1024)S(1)} %fusion.104) | copy-start | bytes 7096
  55.5 47.6 %copy-start.40 = (f32[768]{0:T(1024)}, f32[768]{0:T(1024)S(1)}, u32[]{:S(2)}) copy-start(f32[768]{0:T(1024)S(1)} %get-tuple-element.54) | copy-start | bytes 9220
  80.8 13.7 %copy-start.10 = (bf16[3,197,1,12,64]{1,4,3,0,2:T(8,128)(2,1)}, bf16[3,197,1,12,64]{1,4,3,0,2:T(8,128)(2,1)S(1)}, u32[]{:S(2)}) copy-start(bf16[3,197,1,12,64]{1,4,3,0,2:T(8,128)(2,1)S(1)} %copy.152) | copy-start | bytes 2723332
  115.8 56.9 %all-to-all-start.2 = ((bf16[4,184,1536]{2,1,0:T(8,128)(2,1)}), bf16[4,184,1536]{2,1,0:T(8,128)(2,1)}, u32[]{:S(2)}, u32[]{:S(2)}) async-start(bf16[4,184,1536]{2,1,0:T(8,128)(2,1)} %bitcast.112), calls=%async_computation.2 | async-start | bytes 4521984 | tf_op jit(solution)/shard_map/all_to_all | solution.py:132
  172.8 57.5 %all-to-all-start = ((bf16[4,192,1536]{2,1,0:T(8,128)(2,1)}), bf16[4,192,1536]{2,1,0:T(8,128)(2,1)S(1)}, u32[]{:S(2)}, u32[]{:S(2)}) async-start(bf16[4,192,1536]{2,1,0:T(8,128)(2,1)} %bitcast.10), calls=%async_computation | async-start | bytes 4718592 | tf_op jit(solution)/shard_map/all_to_all | solution.py:132
  176.9 25.8 %copy-start.22 = (bf16[3072,768]{1,0:T(8,128)(2,1)S(1)}, bf16[3072,768]{1,0:T(8,128)(2,1)}, u32[]{:S(2)}) copy-start(bf16[3072,768]{1,0:T(8,128)(2,1)} %reshape_squeeze.3) | copy-start | bytes 14155780
  202.7 15.5 %slice-start.2 = ((s8[9437184]{0:T(1024)(128)(4,1)}), s8[4194304]{0:T(1024)(128)(4,1)S(1)}, s32[]{:S(2)}) async-start(s8[9437184]{0:T(1024)(128)(4,1)} %bitcast.117), calls=%async_computation.13 | async-start | bytes 8388608
  202.7 15.5 %slice-start.3 = ((s8[9437184]{0:T(1024)(128)(4,1)}), s8[4194304]{0:T(1024)(128)(4,1)S(1)}, s32[]{:S(2)}) async-start(s8[9437184]{0:T(1024)(128)(4,1)} %bitcast.117), calls=%async_computation.14 | async-start | bytes 8388608
  230.3 39.1 %copy-start.20 = (bf16[4,192,1536]{2,1,0:T(8,128)(2,1)}, bf16[4,192,1536]{2,1,0:T(8,128)(2,1)S(1)}, u32[]{:S(2)}) copy-start(bf16[4,192,1536]{2,1,0:T(8,128)(2,1)S(1)} %all-to-all-done) | copy-start | bytes 7077892
  230.3 60.8 %all-to-all-start.3 = ((bf16[4,184,1536]{2,1,0:T(8,128)(2,1)}), bf16[4,184,1536]{2,1,0:T(8,128)(2,1)}, u32[]{:S(2)}, u32[]{:S(2)}) async-start(bf16[4,184,1536]{2,1,0:T(8,128)(2,1)} %bitcast.17), calls=%async_computation.3 | async-start | bytes 4521984 | tf_op jit(solution)/shard_map/all_to_all | solution.py:164
  288.6 60.4 %copy-start.59 = (s32[1504]{0:T(1024)S(1)}, s32[1504]{0:T(1024)}, u32[]{:S(2)}) copy-start(s32[1504]{0:T(1024)} %copy-done.58) | copy-start | bytes 18052
  288.6 60.4 %copy-start.63 = (s32[591]{0:T(1024)S(1)}, s32[591]{0:T(1024)}, u32[]{:S(2)}) copy-start(s32[591]{0:T(1024)} %copy-done.62) | copy-start | bytes 7096
  291.1 57.9 %all-to-all-start.1 = ((bf16[4,192,1536]{2,1,0:T(8,128)(2,1)}), bf16[4,192,1536]{2,1,0:T(8,128)(2,1)S(1)}, u32[]{:S(2)}, u32[]{:S(2)}) async-start(bf16[4,192,1536]{2,1,0:T(8,128)(2,1)} %bitcast.13), calls=%async_computation.1 | async-start | bytes 4718592 | tf_op jit(solution)/shard_map/all_to_all | solution.py:164
  296.2 186.6 %reduce-scatter.3.cloned.1.call-start = ((), (), s32[]{:S(2)}) async-start(), calls=%async_computation.8 | async-start | bytes 5529600 | tf_op jit(solution)/shard_map/reduce_scatter | solution.py:251
  429.6 95.2 %all-reduce.3.cloned.1.call-start = ((), (), s32[]{:S(2)}) async-start(), calls=%async_computation.9 | async-start | bytes 1228800 | tf_op jit(solution)/shard_map/psum | solution.py:252
  482.8 121.7 %reduce-scatter.5.cloned.1.call-start = ((), (), s32[]{:S(2)}) async-start(), calls=%async_computation.10 | async-start | bytes 10616832 | tf_op jit(solution)/shard_map/reduce_scatter | solution.py:169
  (56 other events, 255.2 us)
Sparse Core Ops, SparseCore 0:
  11.8 42.3 all-gather.2
  56.6 58.6 all-gather.4
  429.7 52.9 reduce-scatter.2
  484.9 39.7 all-reduce.2
  528.1 76.3 reduce-scatter.4
where the time goes:
time: 624 us; the launch traced here: 615 us
  waiting for transfers between devices  235 us (38%)
  matrix products  195 us (31%)
  local copies, waits for them, and re-layouts  114 us (18%)
  other arithmetic  35.9 us (6%)
  starting transfers between devices  19 us (3%)
  between operations  16.1 us (3%)
    reduce_scatter x1, waiting for transfers between devices, shards(): lax.psum_scatter(expert_grads, 'shard', scatter_dimension=1, tiled=True)  72.8 us
    all_to_all x2, waiting for transfers between devices, shards(): lax.all_to_all(returning, 'expert', split_axis=0, concat_axis=0, tiled=True)  52.4 us
    dot_general x2, matrix products, shards(): jnp.dot(flat_arrived, expert_first, preferred_element_type=jnp.float32)  52.1 us
    all_to_all x2, waiting for transfers between devices, shards(): lax.all_to_all(outgoing[experts * start:experts * (start + size)].reshape...  40.6 us
    all_gather x1, waiting for transfers between devices, shards(): dense_full = lax.all_gather(dense_local, 'shard', axis=0, tiled=True)  32.4 us
    reduce_scatter x1, waiting for transfers between devices, shards(): lax.psum_scatter(dense_grads, 'shard', scatter_dimension=0, tiled=True)  27.7 us
    unnamed x149, local copies, waits for them, and re-layouts  23.7 us
    dot_general x2, matrix products, shards(): lax.dot_general(flat_grad, expert_second, COL_CONTRACT, preferred_element...  22.8 us
  transfers between devices with their start and end apart: 9, of which 7 were waited for; matrix products, arithmetic and copies ran while one was open for 41% of the time, Pallas kernels for 0%

commit v1 on v0

--- a/solution.py
+++ b/solution.py
@@ -9,6 +9,23 @@
 EPSILON = 1e-06
 ROW_CONTRACT = (((0,), (0,)), ((), ()))
 COL_CONTRACT = (((1,), (1,)), ((), ()))
+
+
+def laid_out(parts, dim):
+    parts = jnp.moveaxis(parts, 0, dim)
+    shape = parts.shape
+    return parts.reshape(*shape[:dim], shape[dim] * shape[dim + 1], *shape[dim + 2 :])
+
+
+def gather_around(x, axis, dim):
+    size = lax.axis_size(axis)
+    right = [(i, (i + 1) % size) for i in range(size)]
+    parts = [x]
+    while len(parts) < size:
+        parts.append(lax.ppermute(parts[-1], axis, right))
+    mine = lax.axis_index(axis)
+    parts = jnp.stack(parts)[(mine - jnp.arange(size)) % size]
+    return laid_out(parts, dim)
 
 
 def layer_norm(values, norm_gain):
@@ -56,7 +73,7 @@
     dense_local = jnp.concatenate(
         [w_qkv, w_out, w_router, gain_attn[:, None], gain_moe[:, None]], axis=1
     )
-    dense_full = lax.all_gather(dense_local, "shard", axis=0, tiled=True)
+    dense_full = gather_around(dense_local, "shard", 0)
     full_qkv = dense_full[:, :qkv_cols]
     full_out = dense_full[:, qkv_cols : qkv_cols + width]
     full_router = dense_full[:, qkv_cols + width : qkv_cols + width + n_route]

time: 624 us -> 687 us (1.10)
  waiting for transfers between devices: 235 us -> 292 us
  local copies, waits for them, and re-layouts: 114 us -> 124 us
    ppermute x0 -> x7, waiting for transfers between devices: none -> 93.6 us  [gather_around(): parts.append(lax.ppermute(parts[-1], axis, right))]
    all_gather x1 -> x0, waiting for transfers between devices: 32.4 us -> none  [shards(): dense_full = lax.all_gather(dense_local, 'shard', axis=0, tiled=True)]
    all_to_all x2, waiting for transfers between devices: 40.6 us -> 29.5 us  [shards(): lax.all_to_all(outgoing[experts * start:experts * (start + size)].reshape...]
    unnamed x149 -> x168, local copies, waits for them, and re-layouts: 23.7 us -> 28.4 us
  transfers between devices with their start and end apart: 9 -> 15, of which waited for: 7 -> 13; matrix products, arithmetic and copies ran while one was open for 41% -> 38% of each run, Pallas kernels for 0% -> 0%
where the time goes in v1:
time: 687 us; the launch traced here: 681 us
  waiting for transfers between devices  292 us (43%)
  matrix products  194 us (28%)
  local copies, waits for them, and re-layouts  124 us (18%)
  other arithmetic  34.9 us (5%)
  starting transfers between devices  19.8 us (3%)
  between operations  16.1 us (2%)
    ppermute x7, waiting for transfers between devices, gather_around(): parts.append(lax.ppermute(parts[-1], axis, right))  93.6 us
    reduce_scatter x1, waiting for transfers between devices, shards(): lax.psum_scatter(expert_grads, 'shard', scatter_dimension=1, tiled=True)  72.9 us
    all_to_all x2, waiting for transfers between devices, shards(): lax.all_to_all(returning, 'expert', split_axis=0, concat_axis=0, tiled=True)  52.6 us
    dot_general x2, matrix products, shards(): jnp.dot(flat_arrived, expert_first, preferred_element_type=jnp.float32)  51.9 us
    reduce_scatter x1, waiting for transfers between devices, shards(): lax.psum_scatter(dense_grads, 'shard', scatter_dimension=0, tiled=True)  34.3 us
    all_to_all x2, waiting for transfers between devices, shards(): lax.all_to_all(outgoing[experts * start:experts * (start + size)].reshape...  29.5 us
    unnamed x168, local copies, waits for them, and re-layouts  28.4 us
    dot_general x2, matrix products, shards(): lax.dot_general(flat_grad, expert_second, COL_CONTRACT, preferred_element...  22.8 us
  transfers between devices with their start and end apart: 15, of which 13 were waited for; matrix products, arithmetic and copies ran while one was open for 38% of the time, Pallas kernels for 0%

profile of v1, /device:TPU:0, one launch (start us, length us, event | category | flops | bytes accessed | tf_op | source)
XLA Modules:
  0.0 680.6 jit_solution(17822127153809161348)
XLA Ops:
  24.0 20.8 %collective-permute-done.1 = bf16[96,3078]{1,0:T(8,128)(2,1)S(1)} collective-permute-done((bf16[96,3078]{1,0:T(8,128)(2,1)S(1)}, bf16[96,3078]{1,0:T(8,128)(2,1)S(1)}, u32[]{:S(2)}, u32[]{:S(2)}) %collective-permute-start.1) | collective-permute-done | bytes 591008 | tf_op jit(solution)/shard_map/ppermute | solution.py:25
  45.7 17.9 %collective-permute-done.2 = bf16[96,3078]{1,0:T(8,128)(2,1)S(1)} collective-permute-done((bf16[96,3078]{1,0:T(8,128)(2,1)S(1)}, bf16[96,3078]{1,0:T(8,128)(2,1)S(1)}, u32[]{:S(2)}, u32[]{:S(2)}) %collective-permute-start.2) | collective-permute-done | bytes 591008 | tf_op jit(solution)/shard_map/ppermute | solution.py:25
  64.5 22.7 %collective-permute-done.3 = bf16[96,3078]{1,0:T(8,128)(2,1)S(1)} collective-permute-done((bf16[96,3078]{1,0:T(8,128)(2,1)S(1)}, bf16[96,3078]{1,0:T(8,128)(2,1)S(1)}, u32[]{:S(2)}, u32[]{:S(2)}) %collective-permute-start.3) | collective-permute-done | bytes 591008 | tf_op jit(solution)/shard_map/ppermute | solution.py:25
  88.0 9.6 %collective-permute-done.4 = bf16[96,3078]{1,0:T(8,128)(2,1)S(1)} collective-permute-done((bf16[96,3078]{1,0:T(8,128)(2,1)S(1)}, bf16[96,3078]{1,0:T(8,128)(2,1)S(1)}, u32[]{:S(2)}, u32[]{:S(2)}) %collective-permute-start.4) | collective-permute-done | bytes 591008 | tf_op jit(solution)/shard_map/ppermute | solution.py:25
  98.5 9.5 %collective-permute-done.5 = bf16[96,3078]{1,0:T(8,128)(2,1)S(1)} collective-permute-done((bf16[96,3078]{1,0:T(8,128)(2,1)S(1)}, bf16[96,3078]{1,0:T(8,128)(2,1)S(1)}, u32[]{:S(2)}, u32[]{:S(2)}) %collective-permute-start.5) | collective-permute-done | bytes 591008 | tf_op jit(solution)/shard_map/ppermute | solution.py:25
  109.5 9.6 %collective-permute-done.6 = bf16[96,3078]{1,0:T(8,128)(2,1)S(1)} collective-permute-done((bf16[96,3078]{1,0:T(8,128)(2,1)S(1)}, bf16[96,3078]{1,0:T(8,128)(2,1)S(1)}, u32[]{:S(2)}, u32[]{:S(2)}) %collective-permute-start.6) | collective-permute-done | bytes 591008 | tf_op jit(solution)/shard_map/ppermute | solution.py:25
  132.9 9.2 %reshape.332 = bf16[3,197,3,12,64]{4,3,2,1,0:T(8,128)(2,1)} reshape(bf16[591,2304]{1,0:T(8,128)(2,1)} %convolution_convert_fusion.1) | data formatting | bytes 5446656 | tf_op jit(solution)/shard_map/reshape | solution.py:90
  199.3 8.5 %reshape_squeeze.3 = bf16[3072,768]{1,0:T(8,128)(2,1)} reshape(bf16[1,768,3072]{2,1,0:T(8,128)(2,1)} %slice.167) | data formatting | bytes 9437184 | tf_op jit(solution)/shard_map/reshape;squeeze | solution.py:86
  207.8 27.6 %all-to-all-done.2 = bf16[4,184,1536]{2,1,0:T(8,128)(2,1)} async-done(((bf16[4,184,1536]{2,1,0:T(8,128)(2,1)}), bf16[4,184,1536]{2,1,0:T(8,128)(2,1)}, u32[]{:S(2)}, u32[]{:S(2)}) %all-to-all-start.2) | async-done | bytes 2261024 | tf_op jit(solution)/shard_map/all_to_all | solution.py:149
  239.2 25.7 %multiply_convert_fusion.1 = (bf16[736,3072]{1,0:T(8,128)(2,1)S(1)}, f32[736,3072]{1,0:T(8,128)}, f32[736,3072]{1,0:T(8,128)}) fusion(bf16[2,768,3072]{2,1,0:T(8,128)(2,1)} %all-gather.2.cloned.1.call-done, bf16[736,1536]{1,0:T(8,128)(2,1)} %bitcast.26), kind=kOutput, calls=%fused_computation.24 | convolution fusion | flops 3619848192 | bytes 28459008 | tf_op jit(solution)/shard_map/dot_general | solution.py:158
  268.7 11.8 %add_convert_fusion.3 = bf16[736,3072]{1,0:T(8,128)(2,1)} fusion(f32[736,3072]{1,0:T(8,128)} %get-tuple-element.71, f32[736,3072]{1,0:T(8,128)} %get-tuple-element.86, bf16[3072,768]{1,0:T(8,128)(2,1)S(1)} %copy-done.22, bf16[736,1536]{1,0:T(8,128)(2,1)} %bitcast.26), kind=kOutput, calls=%fused_computation.23 | convolution fusion | flops 3504537600 | bytes 28459008 | tf_op jit(solution)/shard_map/dot_general | solution.py:164
  295.1 26.2 %multiply_convert_fusion = (bf16[768,3072]{1,0:T(8,128)(2,1)S(1)}, f32[768,3072]{1,0:T(8,128)}, f32[768,3072]{1,0:T(8,128)}) fusion(bf16[2,768,3072]{2,1,0:T(8,128)(2,1)} %all-gather.2.cloned.1.call-done, bf16[768,1536]{1,0:T(8,128)(2,1)S(1)} %bitcast.139), kind=kOutput, calls=%fused_computation.8 | convolution fusion | flops 3777232896 | bytes 29491200 | tf_op jit(solution)/shard_map/dot_general | solution.py:158
  329.4 11.0 %add_convert_fusion.2 = bf16[768,3072]{1,0:T(8,128)(2,1)S(1)} fusion(f32[768,3072]{1,0:T(8,128)} %get-tuple-element.69, f32[768,3072]{1,0:T(8,128)} %get-tuple-element.87, bf16[3072,768]{1,0:T(8,128)(2,1)} %reshape_squeeze.3, bf16[768,1536]{1,0:T(8,128)(2,1)S(1)} %bitcast.140), kind=kOutput, calls=%fused_computation.7 | convolution fusion | flops 3656908800 | bytes 29491200 | tf_op jit(solution)/shard_map/dot_general | solution.py:164
  356.4 52.6 %all-to-all-done.1 = bf16[4,192,1536]{2,1,0:T(8,128)(2,1)S(1)} async-done(((bf16[4,192,1536]{2,1,0:T(8,128)(2,1)}), bf16[4,192,1536]{2,1,0:T(8,128)(2,1)S(1)}, u32[]{:S(2)}, u32[]{:S(2)}) %all-to-all-start.1) | async-done | bytes 2359328 | tf_op jit(solution)/shard_map/all_to_all | solution.py:181
  455.3 9.9 %convert_element_type.172 = bf16[591,2304]{0,1:T(8,128)(2,1)} reshape(bf16[3,197,3,12,64]{1,0,4,3,2:T(4,128)(2,1)} %copy.145) | data formatting | bytes 5446656 | tf_op jit(solution)/shard_map/convert_element_type | solution.py:254
  480.0 8.4 %concatenate.32 = bf16[768,3078]{1,0:T(8,128)(2,1)} concatenate(bf16[768,2304]{1,0:T(8,128)(2,1)} %convolution_convert_fusion, bf16[768,768]{1,0:T(8,128)(2,1)} %convolution_convert_fusion.6, bf16[768,4]{1,0:T(8,128)(2,1)S(1)} %copy.147, bf16[768,1]{1,0:T(8,128)(2,1)S(1)} %broadcast_in_dim.40, bf16[768,1]{1,0:T(8,128)(2,1)S(1)} %broadcast_in_dim.41), dimensions={1} | concatenate | bytes 9455616 | tf_op jit(solution)/shard_map/concatenate | solution.py:265
  496.0 8.7 %fusion.78 = f32[768,3072]{1,0:T(8,128)} fusion(bf16[768,3072]{1,0:T(8,128)(2,1)} %copy-done.23, bf16[768,1536]{1,0:T(8,128)(2,1)S(1)} %bitcast.142), kind=kOutput, calls=%fused_computation.145 | convolution fusion | flops 3623878656 | bytes 15335424 | tf_op jit(solution)/shard_map/dot_general | solution.py:174
  504.7 9.1 %add_convert_fusion = bf16[3072,768]{1,0:T(8,128)(2,1)} fusion(f32[3072,768]{1,0:T(8,128)S(1)} %fusion.72, bf16[736,3072]{1,0:T(8,128)(2,1)} %copy-done.70, bf16[736,1536]{1,0:T(8,128)(2,1)} %bitcast.26), kind=kOutput, calls=%fused_computation.5 | convolution fusion | flops 3477602304 | bytes 19808256 | tf_op jit(solution)/shard_map/dot_general | solution.py:171
  513.8 34.3 %reduce-scatter.3.cloned.1.call-done = bf16[96,3078]{1,0:T(8,128)(2,1)} async-done(((bf16[768,3078]{1,0:T(8,128)(2,1)}), bf16[96,3078]{1,0:T(8,128)(2,1)}) %reduce-scatter.3.cloned.1.call-update) | async-done | bytes 590992 | tf_op jit(solution)/shard_map/reduce_scatter | solution.py:268
  548.2 11.5 %fusion.21 = bf16[1,768,3072]{2,1,0:T(8,128)(2,1)} fusion(f32[768,3072]{1,0:T(8,128)} %fusion.78, bf16[736,3072]{1,0:T(8,128)(2,1)} %add_convert_fusion.3, bf16[736,1536]{1,0:T(8,128)(2,1)} %bitcast.26), kind=kOutput, calls=%fused_computation.61 | convolution fusion | flops 3477602304 | bytes 19808256 | tf_op jit(solution)/shard_map/dot_general | solution.py:174
  559.7 8.7 %stack_reshape.4 = bf16[1,768,3072]{2,1,0:T(8,128)(2,1)} reshape(bf16[3072,768]{1,0:T(8,128)(2,1)} %add_convert_fusion) | data formatting | bytes 9437184 | tf_op jit(solution)/shard_map/stack;reshape | solution.py:183
  568.4 8.4 %pad_maximum_fusion = bf16[2,768,3072]{2,1,0:T(8,128)(2,1)} fusion(bf16[1,768,3072]{2,1,0:T(8,128)(2,1)} %stack_reshape.4, bf16[1,768,3072]{2,1,0:T(8,128)(2,1)} %fusion.21), kind=kLoop, calls=%fused_computation.4 | loop fusion | flops 4718592 | bytes 18874368 | tf_op jit(solution)/shard_map/stack | solution.py:183
  581.6 8.7 %all-reduce.3.cloned.1.call-done = bf16[96,3078]{1,0:T(8,128)(2,1)} async-done(((bf16[96,3078]{1,0:T(8,128)(2,1)}), bf16[96,3078]{1,0:T(8,128)(2,1)}) %all-reduce.3.cloned.1.call-update) | async-done | bytes 590992 | tf_op jit(solution)/shard_map/psum | solution.py:269
  597.2 72.9 %reduce-scatter.5.cloned.1.call-done = bf16[2,96,3072]{2,1,0:T(8,128)(2,1)} async-done(((bf16[2,768,3072]{2,1,0:T(8,128)(2,1)}), bf16[2,96,3072]{2,1,0:T(8,128)(2,1)}) %reduce-scatter.5.cloned.1.call-update) | async-done | bytes 1179664 | tf_op jit(solution)/shard_map/reduce_scatter | solution.py:186
  (310 shorter events, 221.4 us)
Async XLA Ops:
  7.3 187.3 %all-gather.2.cloned.1.call-start = ((), (), s32[]{:S(2)}) async-start(), calls=%async_computation.6 | async-start | bytes 10616832 | tf_op jit(solution)/shard_map/all_gather | solution.py:84
  11.9 11.2 %collective-permute-start = (bf16[96,3078]{1,0:T(8,128)(2,1)S(1)}, bf16[96,3078]{1,0:T(8,128)(2,1)S(1)}, u32[]{:S(2)}, u32[]{:S(2)}) collective-permute-start(bf16[96,3078]{1,0:T(8,128)(2,1)S(1)} %concatenate.26), channel_id=1, source_target_pairs={{0,1},{1,2},{2,3},{3,4},{4,5},{5,6},{6,7},{7,0},{8,9},{9,10},{10,1... | collective-permute-start | bytes 1772936 | tf_op jit(solution)/shard_map/ppermute | solution.py:25
  16.9 162.5 %copy-start.62 = (s32[591]{0:T(1024)}, s32[591]{0:T(1024)S(1)}, u32[]{:S(2)}) copy-start(s32[591]{0:T(1024)S(1)} %get-tuple-element.65) | copy-start | bytes 7096
  16.9 164.7 %copy-start.64 = (s32[591]{0:T(1024)}, s32[591]{0:T(1024)S(1)}, u32[]{:S(2)}) copy-start(s32[591]{0:T(1024)S(1)} %get-tuple-element.64) | copy-start | bytes 7096
  17.2 159.2 %copy-start.31 = (f32[591]{0:T(1024)}, f32[591]{0:T(1024)S(1)}, u32[]{:S(2)}) copy-start(f32[591]{0:T(1024)S(1)} %fusion.106) | copy-start | bytes 7096
  17.5 109.4 %copy-start.48 = (f32[591]{0:T(1024)}, f32[591]{0:T(1024)S(1)}, u32[]{:S(2)}) copy-start(f32[591]{0:T(1024)S(1)} %broadcast_multiply_fusion.2) | copy-start | bytes 7096
  17.9 91.6 %copy-start.52 = (f32[591]{0:T(1024)}, f32[591]{0:T(1024)S(1)}, u32[]{:S(2)}) copy-start(f32[591]{0:T(1024)S(1)} %fusion.53) | copy-start | bytes 7096
  17.9 163.7 %copy-start.60 = (s32[1504]{0:T(1024)}, s32[1504]{0:T(1024)S(1)}, u32[]{:S(2)}) copy-start(s32[1504]{0:T(1024)S(1)} %pad_add_fusion) | copy-start | bytes 18052
  18.0 108.9 %copy-start.58 = (f32[591]{0:T(1024)}, f32[591]{0:T(1024)S(1)}, u32[]{:S(2)}) copy-start(f32[591]{0:T(1024)S(1)} %fusion.104) | copy-start | bytes 7096
  23.1 21.7 %collective-permute-start.1 = (bf16[96,3078]{1,0:T(8,128)(2,1)S(1)}, bf16[96,3078]{1,0:T(8,128)(2,1)S(1)}, u32[]{:S(2)}, u32[]{:S(2)}) collective-permute-start(bf16[96,3078]{1,0:T(8,128)(2,1)S(1)} %collective-permute-done), channel_id=1, source_target_pairs={{0,1},{1,2},{2,3},{3,4},{4,5},{5,6},{6,7},{7,0},{8,9},{9,10},{10,1... | collective-permute-start | bytes 1772936 | tf_op jit(solution)/shard_map/ppermute | solution.py:25
  44.8 18.8 %collective-permute-start.2 = (bf16[96,3078]{1,0:T(8,128)(2,1)S(1)}, bf16[96,3078]{1,0:T(8,128)(2,1)S(1)}, u32[]{:S(2)}, u32[]{:S(2)}) collective-permute-start(bf16[96,3078]{1,0:T(8,128)(2,1)S(1)} %collective-permute-done.1), channel_id=1, source_target_pairs={{0,1},{1,2},{2,3},{3,4},{4,5},{5,6},{6,7},{7,0},{8,9},{9,10},{10,1... | collective-permute-start | bytes 1772936 | tf_op jit(solution)/shard_map/ppermute | solution.py:25
  63.6 23.5 %collective-permute-start.3 = (bf16[96,3078]{1,0:T(8,128)(2,1)S(1)}, bf16[96,3078]{1,0:T(8,128)(2,1)S(1)}, u32[]{:S(2)}, u32[]{:S(2)}) collective-permute-start(bf16[96,3078]{1,0:T(8,128)(2,1)S(1)} %collective-permute-done.2), channel_id=1, source_target_pairs={{0,1},{1,2},{2,3},{3,4},{4,5},{5,6},{6,7},{7,0},{8,9},{9,10},{10,1... | collective-permute-start | bytes 1772936 | tf_op jit(solution)/shard_map/ppermute | solution.py:25
  87.1 10.5 %collective-permute-start.4 = (bf16[96,3078]{1,0:T(8,128)(2,1)S(1)}, bf16[96,3078]{1,0:T(8,128)(2,1)S(1)}, u32[]{:S(2)}, u32[]{:S(2)}) collective-permute-start(bf16[96,3078]{1,0:T(8,128)(2,1)S(1)} %collective-permute-done.3), channel_id=1, source_target_pairs={{0,1},{1,2},{2,3},{3,4},{4,5},{5,6},{6,7},{7,0},{8,9},{9,10},{10,1... | collective-permute-start | bytes 1772936 | tf_op jit(solution)/shard_map/ppermute | solution.py:25
  97.6 10.5 %collective-permute-start.5 = (bf16[96,3078]{1,0:T(8,128)(2,1)S(1)}, bf16[96,3078]{1,0:T(8,128)(2,1)S(1)}, u32[]{:S(2)}, u32[]{:S(2)}) collective-permute-start(bf16[96,3078]{1,0:T(8,128)(2,1)S(1)} %collective-permute-done.4), channel_id=1, source_target_pairs={{0,1},{1,2},{2,3},{3,4},{4,5},{5,6},{6,7},{7,0},{8,9},{9,10},{10,1... | collective-permute-start | bytes 1772936 | tf_op jit(solution)/shard_map/ppermute | solution.py:25
  108.1 11.0 %collective-permute-start.6 = (bf16[96,3078]{1,0:T(8,128)(2,1)S(1)}, bf16[96,3078]{1,0:T(8,128)(2,1)S(1)}, u32[]{:S(2)}, u32[]{:S(2)}) collective-permute-start(bf16[96,3078]{1,0:T(8,128)(2,1)S(1)} %collective-permute-done.5), channel_id=1, source_target_pairs={{0,1},{1,2},{2,3},{3,4},{4,5},{5,6},{6,7},{7,0},{8,9},{9,10},{10,1... | collective-permute-start | bytes 1772936 | tf_op jit(solution)/shard_map/ppermute | solution.py:25
  187.1 48.3 %all-to-all-start.2 = ((bf16[4,184,1536]{2,1,0:T(8,128)(2,1)}), bf16[4,184,1536]{2,1,0:T(8,128)(2,1)}, u32[]{:S(2)}, u32[]{:S(2)}) async-start(bf16[4,184,1536]{2,1,0:T(8,128)(2,1)} %bitcast.131), calls=%async_computation.2 | async-start | bytes 4521984 | tf_op jit(solution)/shard_map/all_to_all | solution.py:149
  235.4 54.7 %all-to-all-start = ((bf16[4,192,1536]{2,1,0:T(8,128)(2,1)}), bf16[4,192,1536]{2,1,0:T(8,128)(2,1)S(1)}, u32[]{:S(2)}, u32[]{:S(2)}) async-start(bf16[4,192,1536]{2,1,0:T(8,128)(2,1)} %bitcast.20), calls=%async_computation | async-start | bytes 4718592 | tf_op jit(solution)/shard_map/all_to_all | solution.py:149
  290.1 61.0 %all-to-all-start.3 = ((bf16[4,184,1536]{2,1,0:T(8,128)(2,1)}), bf16[4,184,1536]{2,1,0:T(8,128)(2,1)}, u32[]{:S(2)}, u32[]{:S(2)}) async-start(bf16[4,184,1536]{2,1,0:T(8,128)(2,1)} %bitcast.27), calls=%async_computation.3 | async-start | bytes 4521984 | tf_op jit(solution)/shard_map/all_to_all | solution.py:181
  348.6 60.4 %copy-start.61 = (s32[1504]{0:T(1024)S(1)}, s32[1504]{0:T(1024)}, u32[]{:S(2)}) copy-start(s32[1504]{0:T(1024)} %copy-done.60) | copy-start | bytes 18052
  348.6 60.4 %copy-start.65 = (s32[591]{0:T(1024)S(1)}, s32[591]{0:T(1024)}, u32[]{:S(2)}) copy-start(s32[591]{0:T(1024)} %copy-done.64) | copy-start | bytes 7096
  351.1 57.9 %all-to-all-start.1 = ((bf16[4,192,1536]{2,1,0:T(8,128)(2,1)}), bf16[4,192,1536]{2,1,0:T(8,128)(2,1)S(1)}, u32[]{:S(2)}, u32[]{:S(2)}) async-start(bf16[4,192,1536]{2,1,0:T(8,128)(2,1)} %bitcast.23), calls=%async_computation.1 | async-start | bytes 4718592 | tf_op jit(solution)/shard_map/all_to_all | solution.py:181
  356.2 192.0 %reduce-scatter.3.cloned.1.call-start = ((), (), s32[]{:S(2)}) async-start(), calls=%async_computation.7 | async-start | bytes 5529600 | tf_op jit(solution)/shard_map/reduce_scatter | solution.py:268
  488.5 101.8 %all-reduce.3.cloned.1.call-start = ((), (), s32[]{:S(2)}) async-start(), calls=%async_computation.8 | async-start | bytes 1228800 | tf_op jit(solution)/shard_map/psum | solution.py:269
  548.1 121.9 %reduce-scatter.5.cloned.1.call-start = ((), (), s32[]{:S(2)}) async-start(), calls=%async_computation.9 | async-start | bytes 10616832 | tf_op jit(solution)/shard_map/reduce_scatter | solution.py:186
  (67 other events, 394.8 us)
Sparse Core Ops, SparseCore 0:
  11.3 78.3 all-gather.1
  488.6 59.4 reduce-scatter.2
  550.5 39.7 all-reduce.2
  593.6 76.3 reduce-scatter.4
